TPU v7x, 128 devices: a whole 4x4x4 slice. The times are simulated.
128 devices in a mesh: node: 8 (over x, core), dev: 16 (over z, y).
Axes of the slice: x: 4, y: 4, z: 4, core: 2. Of those that a mesh axis runs over, the one named last changes fastest.
Arguments:
- tokens: bfloat16 [32768, 7168], P(('node', 'dev')), may hold values from -6 to 6
- grad_out: bfloat16 [32768, 7168], P(('node', 'dev')), may hold values from -1.796875 to 1.796875
- router_gates: bfloat16 [32768, 8], P(('node', 'dev')), may hold values from 0.049804688 to 1
- expert_ids: int32 [32768, 8], P(('node', 'dev')), may hold values from 0 to 255, as said below
- slot_plan: int32 [256, 2], replicated, may hold values from 0 to 16, as said below
- w_gate: bfloat16 [8, 7168, 2048], P(None, 'dev', 'node'), may hold values from -0.0625 to 0.0625
- w_up: bfloat16 [8, 7168, 2048], P(None, 'dev', 'node'), may hold values from -0.0625 to 0.0625
- w_down: bfloat16 [8, 2048, 7168], P(None, 'node', 'dev'), may hold values from -0.125 to 0.125
Outputs:
- grad_tokens: bfloat16 [32768, 7168], P(('node', 'dev'))
- grad_gates: float32 [32768, 8], P(('node', 'dev'))
- grad_w_gate: bfloat16 [8, 7168, 2048], P(None, 'dev', 'node')
- grad_w_up: bfloat16 [8, 7168, 2048], P(None, 'dev', 'node')
- grad_w_down: bfloat16 [8, 2048, 7168], P(None, 'node', 'dev')
Inputs may be any that keep to these rules, and one draw needn't show every extreme that they name: `expert_ids`: each token names 8 different experts. Within one block of 256 tokens (the tokens of one device), at most 4 pairs name any one expert that has slots, and in every draw one expert that has slots is named exactly 2 * 2 times in every block. `slot_plan`: exactly 8 rows hold slots: each such row holds two different slots, and every slot 0 .. 15 stands in exactly one row. Every entry of the other rows equals 16.
All inputs are finite; a program needn't handle non-finite values.
Results may differ from a plain program's by a relative error of at most 0.0059.
Values may be sent and summed in bfloat16 or wider, within the bound.
No kernel may reach another device: no remote copies, remote signals or barrier semaphores. Data moves between devices by JAX's collectives and lax.ppermute only.
A program may use at most 128 MiB of HBM per device.

v0:
```python
import jax
import jax.numpy as jnp
from jax import lax
from jax.sharding import PartitionSpec as P

EXPERTS = 256
TOP = 8
CAP = 2


def expert_pass(pieces, slot_gate, slot_up, slot_down):
    x_piece, dy_piece, gate_piece = pieces
    lead_count = x_piece.shape[0]
    slot_count = slot_down.shape[0]
    model_width = x_piece.shape[-1]
    x_rows = x_piece.reshape(-1, model_width)
    dy_split = dy_piece.reshape(-1, slot_count, model_width // slot_count)
    gate_rows = gate_piece.reshape(-1, 1).astype(jnp.float32)
    gate_pre = jnp.dot(x_rows, slot_gate, preferred_element_type=jnp.float32)
    up_pre = jnp.dot(x_rows, slot_up, preferred_element_type=jnp.float32)
    back_proj = jnp.einsum("rsk,shk->rh", dy_split, slot_down, preferred_element_type=jnp.float32)
    sigmoid_gate = jax.nn.sigmoid(gate_pre)
    active = gate_pre * sigmoid_gate
    hidden = active * up_pre
    scaled_back = gate_rows * back_proj
    d_gate = (scaled_back * up_pre * sigmoid_gate * (1.0 + gate_pre * (1.0 - sigmoid_gate))).astype(
        jnp.bfloat16
    )
    d_up = (scaled_back * active).astype(jnp.bfloat16)
    scaled_hidden = (gate_rows * hidden).astype(jnp.bfloat16)
    gate_terms = jnp.sum(back_proj * hidden, axis=-1)
    row_terms = jnp.einsum("rh,dh->rd", d_gate, slot_gate, preferred_element_type=jnp.float32)
    row_terms = row_terms + jnp.einsum(
        "rh,dh->rd", d_up, slot_up, preferred_element_type=jnp.float32
    )
    acc_gate = jnp.einsum("rd,rh->dh", x_rows, d_gate, preferred_element_type=jnp.float32)
    acc_up = jnp.einsum("rd,rh->dh", x_rows, d_up, preferred_element_type=jnp.float32)
    acc_down = jnp.einsum(
        "rsk,rh->shk", dy_split, scaled_hidden, preferred_element_type=jnp.float32
    )
    row_acc = row_terms.reshape(lead_count, slot_count, -1, model_width)
    gate_acc = gate_terms.reshape(lead_count, slot_count, -1)
    return (acc_gate, acc_up, acc_down, row_acc, gate_acc)


def local(tokens, grad_out, router_gates, expert_ids, slot_plan, w_gate, w_up, w_down):
    slot_count = lax.axis_size("dev")
    tok_rows, model_width = tokens.shape
    hidden_width = w_gate.shape[2]
    round_total = w_gate.shape[0]
    pair_total = tok_rows * TOP
    expert_match = expert_ids[:, :, None] == jnp.arange(EXPERTS, dtype=jnp.int32)
    first_slot = jnp.sum(jnp.where(expert_match, slot_plan[:, 0], 0), axis=-1).reshape(pair_total)
    second_slot = jnp.sum(jnp.where(expert_match, slot_plan[:, 1], 0), axis=-1).reshape(pair_total)
    is_live = first_slot < slot_count
    first_hot = (first_slot[:, None] == jnp.arange(slot_count, dtype=jnp.int32)[None, :]).astype(
        jnp.int32
    )
    pair_order = jnp.sum(first_hot * (jnp.cumsum(first_hot, axis=0) - 1), axis=-1)
    pair_slot = jnp.where(pair_order % 2 == 0, first_slot, second_slot)
    target_row = pair_slot * CAP + pair_order // 2
    position_ids = jnp.arange(slot_count * CAP, dtype=jnp.int32)
    chooser = (is_live[None, :] & (target_row[None, :] == position_ids[:, None])).astype(
        jnp.float32
    )
    pick_rows = jnp.sum(chooser.reshape(slot_count * CAP, tok_rows, TOP), axis=-1)
    pick_half = pick_rows.astype(jnp.bfloat16)
    x_send = (
        jnp.dot(pick_half, tokens, preferred_element_type=jnp.float32)
        .astype(jnp.bfloat16)
        .reshape(slot_count, CAP, model_width)
    )
    dy_send = (
        jnp.dot(pick_half, grad_out, preferred_element_type=jnp.float32)
        .astype(jnp.bfloat16)
        .reshape(slot_count, CAP, model_width)
    )
    flat_gates = router_gates.reshape(pair_total).astype(jnp.float32)
    gate_send = (
        jnp.dot(chooser, flat_gates, precision=lax.Precision.HIGHEST)
        .astype(jnp.bfloat16)
        .reshape(slot_count, CAP)
    )
    in_round = (slot_plan[:, 0] < slot_count).astype(jnp.int32)
    expert_rank = jnp.cumsum(in_round) - 1
    holder = jnp.any(slot_plan[:, :, None] == jnp.arange(slot_count, dtype=jnp.int32), axis=1)
    slot_rank = jnp.sum(jnp.where(holder, expert_rank[:, None], 0), axis=0)
    grouping = (slot_rank[None, :] == jnp.arange(round_total, dtype=jnp.int32)[:, None]).astype(
        jnp.bfloat16
    )
    copy_gate = jnp.take(w_gate, slot_rank, axis=0)
    copy_up = jnp.take(w_up, slot_rank, axis=0)
    copy_down = jnp.take(w_down, slot_rank, axis=0)
    slot_gate, slot_up, slot_down = (
        lax.all_to_all(copy_gate, "dev", split_axis=0, concat_axis=0, tiled=True),
        lax.all_to_all(copy_up, "dev", split_axis=0, concat_axis=0, tiled=True),
        lax.all_to_all(copy_down, "dev", split_axis=0, concat_axis=0, tiled=True),
    )
    slot_gate = slot_gate.reshape(model_width, hidden_width)
    slot_up = slot_up.reshape(model_width, hidden_width)
    got_x, got_dy, got_gate = (
        lax.all_to_all(x_send, "dev", split_axis=0, concat_axis=0, tiled=True),
        lax.all_to_all(dy_send, "dev", split_axis=0, concat_axis=0, tiled=True),
        lax.all_to_all(gate_send, "dev", split_axis=0, concat_axis=0, tiled=True),
    )
    totals = expert_pass(
        (
            lax.all_gather(got_x[None], "node", axis=0, tiled=True),
            lax.all_gather(got_dy[None], "node", axis=0, tiled=True),
            lax.all_gather(got_gate[None], "node", axis=0, tiled=True),
        ),
        slot_gate,
        slot_up,
        slot_down,
    )
    acc_gate, acc_up, acc_down, row_acc, gate_acc = totals
    summed_rows, summed_gates = (
        lax.psum_scatter(row_acc, "node", scatter_dimension=0, tiled=True),
        lax.psum_scatter(gate_acc, "node", scatter_dimension=0, tiled=True),
    )
    back_rows, back_gates = (
        lax.all_to_all(summed_rows, "dev", split_axis=1, concat_axis=1, tiled=True),
        lax.all_to_all(summed_gates, "dev", split_axis=1, concat_axis=1, tiled=True),
    )
    grad_tokens = jnp.einsum(
        "qt,qd->td",
        pick_rows,
        back_rows.reshape(slot_count * CAP, model_width),
        precision=lax.Precision.HIGHEST,
    ).astype(jnp.bfloat16)
    grad_gates = jnp.dot(
        back_gates.reshape(slot_count * CAP), chooser, precision=lax.Precision.HIGHEST
    ).reshape(tok_rows, TOP)
    send_gate = acc_gate.astype(jnp.bfloat16).reshape(
        slot_count, model_width // slot_count, hidden_width
    )
    send_up = acc_up.astype(jnp.bfloat16).reshape(
        slot_count, model_width // slot_count, hidden_width
    )
    send_down = acc_down.astype(jnp.bfloat16)
    got_wgate, got_wup, got_wdown = (
        lax.all_to_all(send_gate, "dev", split_axis=0, concat_axis=0, tiled=True),
        lax.all_to_all(send_up, "dev", split_axis=0, concat_axis=0, tiled=True),
        lax.all_to_all(send_down, "dev", split_axis=0, concat_axis=0, tiled=True),
    )
    grad_w_gate = jnp.einsum(
        "js,sdh->jdh", grouping, got_wgate, preferred_element_type=jnp.float32
    ).astype(jnp.bfloat16)
    grad_w_up = jnp.einsum(
        "js,sdh->jdh", grouping, got_wup, preferred_element_type=jnp.float32
    ).astype(jnp.bfloat16)
    grad_w_down = jnp.einsum(
        "js,shk->jhk", grouping, got_wdown, preferred_element_type=jnp.float32
    ).astype(jnp.bfloat16)
    return (grad_tokens, grad_gates, grad_w_gate, grad_w_up, grad_w_down)


def solution(mesh):
    return jax.shard_map(
        local,
        mesh=mesh,
        in_specs=(
            P(("node", "dev"), None),
            P(("node", "dev"), None),
            P(("node", "dev"), None),
            P(("node", "dev"), None),
            P(),
            P(None, "dev", "node"),
            P(None, "dev", "node"),
            P(None, "node", "dev"),
        ),
        out_specs=(
            P(("node", "dev"), None),
            P(("node", "dev"), None),
            P(None, "dev", "node"),
            P(None, "dev", "node"),
            P(None, "node", "dev"),
        ),
        check_vma=False,
    )
```

profile of v0, /device:TPU:14, one launch (start us, length us, event | category | flops | bytes accessed | tf_op | source)
XLA Modules:
  0.0 506.6 jit_solution(3346200505427443808)
XLA Ops:
  8.9 9.2 %select_reduce_fusion = (s32[256,8]{1,0:T(8,128)S(1)}, s32[256,8]{1,0:T(8,128)S(1)}) fusion(s32[256]{0:T(256)S(1)} %bitcast.78, s32[256,8]{1,0:T(8,128)S(1)} %copy.90, s32[256]{0:T(256)S(1)} %bitcast.77), kind=kLoop, calls=%fused_computation.21 | loop fusion | flops 2617344 | bytes 26624 | tf_op jit(solution)/shard_map/reduce_sum | solution.py:54
  27.2 17.7 %all_to_all.60 = bf16[16,2,7168]{2,1,0:T(2,128)(2,1)} all-to-all(bf16[16,2,7168]{2,1,0:T(2,128)(2,1)S(1)} %reshape.235), channel_id=1, replica_groups=mesh['node'=8,'dev'=16] {'dev'}, dimensions={0} | all-to-all | bytes 917504 | tf_op jit(solution)/shard_map/all_to_all | solution.py:102
  62.3 7.3 %all-to-all-start.1 = ((bf16[16,2,7168]{2,1,0:T(2,128)(2,1)}), bf16[16,2,7168]{2,1,0:T(2,128)(2,1)S(1)}, u32[]{:S(2)}, u32[]{:S(2)}) async-start(bf16[16,2,7168]{2,1,0:T(2,128)(2,1)} %reshape.232), calls=%async_computation.1 | async-start | bytes 917504 | tf_op jit(solution)/shard_map/all_to_all | solution.py:103
  85.4 44.8 %all-to-all-done.5 = bf16[16,448,256]{2,1,0:T(8,128)(2,1)} async-done(((bf16[16,448,256]{2,1,0:T(8,128)(2,1)}), bf16[16,448,256]{2,1,0:T(8,128)(2,1)}, u32[]{:S(2)}, u32[]{:S(2)}) %all-to-all-start.5) | async-done | bytes 3670048 | tf_op jit(solution)/shard_map/all_to_all | solution.py:95
  130.2 9.0 %all-to-all-start.4 = ((bf16[16,448,256]{2,1,0:T(8,128)(2,1)}), bf16[16,448,256]{2,1,0:T(8,128)(2,1)}, u32[]{:S(2)}, u32[]{:S(2)}) async-start(bf16[16,448,256]{2,1,0:T(8,128)(2,1)} %get-tuple-element.43), calls=%async_computation.4 | async-start | bytes 7340032 | tf_op jit(solution)/shard_map/all_to_all | solution.py:96
  146.2 38.6 %all-to-all-done.4 = bf16[16,448,256]{2,1,0:T(8,128)(2,1)} async-done(((bf16[16,448,256]{2,1,0:T(8,128)(2,1)}), bf16[16,448,256]{2,1,0:T(8,128)(2,1)}, u32[]{:S(2)}, u32[]{:S(2)}) %all-to-all-start.4) | async-done | bytes 3670048 | tf_op jit(solution)/shard_map/all_to_all | solution.py:96
  184.7 8.8 %all-to-all-start.2 = ((bf16[16,256,448]{1,2,0:T(8,128)(2,1)}), bf16[16,256,448]{1,2,0:T(8,128)(2,1)}, u32[]{:S(2)}, u32[]{:S(2)}) async-start(bf16[16,256,448]{1,2,0:T(8,128)(2,1)} %broadcast_select_fusion.2), calls=%async_computation.2 | async-start | bytes 7340032 | tf_op jit(solution)/shard_map/all_to_all | solution.py:97
  193.6 13.0 %all-gather = bf16[128,1,2]{2,1,0:T(2,128)(2,1)S(1)} all-gather(bf16[16,1,2]{2,1,0:T(2,128)(2,1)S(1)} %all-to-all-done), channel_id=2, replica_groups=mesh['node'=8,'dev'=16] {'node'}, dimensions={0}, use_global_device_ids=true | all-gather | bytes 576 | tf_op jit(solution)/shard_map/all_gather | solution.py:110
  206.9 8.4 %reshape.236 = bf16[256,7168]{1,0:T(8,128)(2,1)} reshape(bf16[128,2,7168]{2,1,0:T(2,128)(2,1)} %all-gather.8.cloned.1.call-done) | data formatting | bytes 7340032 | tf_op jit(solution)/shard_map/reshape | solution.py:16
  215.3 9.6 %reshape.233 = bf16[256,16,448]{2,1,0:T(8,128)(2,1)} reshape(bf16[128,2,7168]{2,1,0:T(2,128)(2,1)} %all-gather.6.cloned.1.call-done) | data formatting | bytes 7340032 | tf_op jit(solution)/shard_map/reshape | solution.py:17
  239.1 8.3 %multiply_reduce_fusion = (f32[256]{0:T(256)S(1)}, bf16[256,256]{0,1:T(8,128)(2,1)S(1)}, bf16[256,256]{0,1:T(8,128)(2,1)S(1)}) fusion(f32[256,256]{0,1:T(8,128)S(1)} %fusion.61, f32[256,256]{0,1:T(8,128)S(1)} %fusion.62, f32[256]{0:T(256)S(1)} %reshape.245, bf16[16,256,448]{1,2,0:T(8,128)(2,1)} %all-to-all-done.2, bf16[256,16,448]{2,1,0:T(8,128)(2,1)} %reshape.233), kind=kOutput, calls=%fused_computation.32 | convolution fusion | flops 940637952 | bytes 8128512 | tf_op jit(solution)/shard_map/rsk,shk->rh/dot_general | solution.py:21
  254.5 8.3 %convolution_add_fusion = f32[256,7168]{1,0:T(8,128)} fusion(f32[256,7168]{1,0:T(8,128)} %fusion.63, bf16[256,256]{0,1:T(8,128)(2,1)S(1)} %get-tuple-element.40, bf16[7168,256]{1,0:T(8,128)(2,1)} %bitcast.9), kind=kOutput, calls=%fused_computation.3 | convolution fusion | flops 941359104 | bytes 18481152 | tf_op jit(solution)/shard_map/rh,dh->rd/dot_general | solution.py:33
  262.8 9.7 %reshape.239 = f32[8,16,2,7168]{3,2,1,0:T(2,128)} reshape(f32[256,7168]{1,0:T(8,128)} %convolution_add_fusion) | data formatting | bytes 14680064 | tf_op jit(solution)/shard_map/reshape | solution.py:41
  272.6 8.3 %copy.96 = f32[8,16,2,7168]{3,1,2,0:T(8,128)} copy(f32[8,16,2,7168]{3,2,1,0:T(2,128)} %reshape.239) | data formatting | bytes 14680064 | tf_op jit(solution)/shard_map/reshape | solution.py:41
  280.9 8.5 %copy.103 = bf16[256,16,448]{0,1,2:T(8,128)(2,1)} copy(bf16[256,16,448]{2,1,0:T(8,128)(2,1)} %reshape.233) | data formatting | bytes 7340032 | tf_op jit(solution)/shard_map/reshape | solution.py:17
  289.4 8.9 %all-to-all-start.7 = ((f32[1,16,2]{2,0,1:T(1,128)}), f32[1,16,2]{2,0,1:T(1,128)S(1)}, u32[]{:S(2)}, u32[]{:S(2)}) async-start(f32[1,16,2]{2,0,1:T(1,128)} %bitcast.76), calls=%async_computation.9 | async-start | bytes 16384 | tf_op jit(solution)/shard_map/all_to_all | solution.py:123
  304.8 7.3 %all-to-all-start.10 = ((bf16[16,256,448]{1,2,0:T(8,128)(2,1)}), bf16[16,256,448]{1,2,0:T(8,128)(2,1)}, u32[]{:S(2)}, u32[]{:S(2)}) async-start(bf16[16,256,448]{1,2,0:T(8,128)(2,1)} %copy.104), calls=%async_computation.12 | async-start | bytes 7340032 | tf_op jit(solution)/shard_map/all_to_all | solution.py:144
  317.2 39.1 %all-to-all-done.10 = bf16[16,256,448]{1,2,0:T(8,128)(2,1)} async-done(((bf16[16,256,448]{1,2,0:T(8,128)(2,1)}), bf16[16,256,448]{1,2,0:T(8,128)(2,1)}, u32[]{:S(2)}, u32[]{:S(2)}) %all-to-all-start.10) | async-done | bytes 3670048 | tf_op jit(solution)/shard_map/all_to_all | solution.py:144
  356.3 8.1 %all-to-all-start.8 = ((bf16[16,448,256]{2,1,0:T(8,128)(2,1)}), bf16[16,448,256]{2,1,0:T(8,128)(2,1)}, u32[]{:S(2)}, u32[]{:S(2)}) async-start(bf16[16,448,256]{2,1,0:T(8,128)(2,1)} %bitcast.72), calls=%async_computation.10 | async-start | bytes 7340032 | tf_op jit(solution)/shard_map/all_to_all | solution.py:142
  369.5 41.6 %all-to-all-done.8 = bf16[16,448,256]{2,1,0:T(8,128)(2,1)} async-done(((bf16[16,448,256]{2,1,0:T(8,128)(2,1)}), bf16[16,448,256]{2,1,0:T(8,128)(2,1)}, u32[]{:S(2)}, u32[]{:S(2)}) %all-to-all-start.8) | async-done | bytes 3670048 | tf_op jit(solution)/shard_map/all_to_all | solution.py:142
  411.0 9.3 %all-to-all-start.9 = ((bf16[16,448,256]{2,1,0:T(8,128)(2,1)}), bf16[16,448,256]{2,1,0:T(8,128)(2,1)}, u32[]{:S(2)}, u32[]{:S(2)}) async-start(bf16[16,448,256]{2,1,0:T(8,128)(2,1)} %bitcast.71), calls=%async_computation.11 | async-start | bytes 7340032 | tf_op jit(solution)/shard_map/all_to_all | solution.py:143
  426.3 38.1 %all-to-all-done.9 = bf16[16,448,256]{2,1,0:T(8,128)(2,1)} async-done(((bf16[16,448,256]{2,1,0:T(8,128)(2,1)}), bf16[16,448,256]{2,1,0:T(8,128)(2,1)}, u32[]{:S(2)}, u32[]{:S(2)}) %all-to-all-start.9) | async-done | bytes 3670048 | tf_op jit(solution)/shard_map/all_to_all | solution.py:143
  464.4 7.9 %all-to-all-start.6 = ((f32[1,16,2,7168]{3,2,0,1:T(2,128)}), f32[1,16,2,7168]{3,2,0,1:T(2,128)S(1)}, u32[]{:S(2)}, u32[]{:S(2)}) async-start(f32[1,16,2,7168]{3,2,0,1:T(2,128)} %copy.97), calls=%async_computation.7 | async-start | bytes 1835008 | tf_op jit(solution)/shard_map/all_to_all | solution.py:122
  491.4 8.5 %convolution_convert_fusion.2 = bf16[256,7168]{1,0:T(8,128)(2,1)} fusion(f32[32,256]{1,0:T(8,128)S(1)} %convert_reduce_fusion, f32[32,7168]{1,0:T(8,128)} %reshape.240), kind=kOutput, calls=%fused_computation.6 | convolution fusion | flops 706478080 | bytes 4620288 | tf_op jit(solution)/shard_map/qt,qd->td/dot_general | solution.py:125
  (101 shorter events, 114.1 us)
Async XLA Ops:
  7.2 44.6 %copy-start = (bf16[8,448,256]{2,1,0:T(8,128)(2,1)S(1)}, bf16[8,448,256]{2,1,0:T(8,128)(2,1)}, u32[]{:S(2)}) copy-start(bf16[8,448,256]{2,1,0:T(8,128)(2,1)} %param.16) | copy-start | bytes 5505028
  7.2 199.7 %all-gather.8.cloned.1.call-start = ((), (), s32[]{:S(2)}) async-start(), calls=%async_computation.16 | async-start | bytes 4128768 | tf_op jit(solution)/shard_map/all_gather | solution.py:108
  23.9 21.2 %copy-start.6 = (bf16[256,8]{0,1:T(8,128)(2,1)S(1)}, bf16[256,8]{0,1:T(8,128)(2,1)}, u32[]{:S(2)}) copy-start(bf16[256,8]{0,1:T(8,128)(2,1)} %param.12) | copy-start | bytes 12292
  24.0 26.9 %copy-start.5 = (s32[256,2]{0,1:T(2,128)S(1)}, s32[256,2]{0,1:T(2,128)}, u32[]{:S(2)}) copy-start(s32[256,2]{0,1:T(2,128)} %param.14) | copy-start | bytes 6148
  46.2 16.1 %all-to-all-start = ((bf16[16,1,2]{2,1,0:T(2,128)(2,1)}), bf16[16,1,2]{2,1,0:T(2,128)(2,1)S(1)}, u32[]{:S(2)}, u32[]{:S(2)}) async-start(bf16[16,1,2]{2,1,0:T(2,128)(2,1)} %all_to_all.48), calls=%async_computation | async-start | bytes 16384 | tf_op jit(solution)/shard_map/all_to_all | solution.py:104
  62.3 15.7 %all-to-all-start.1 = ((bf16[16,2,7168]{2,1,0:T(2,128)(2,1)}), bf16[16,2,7168]{2,1,0:T(2,128)(2,1)S(1)}, u32[]{:S(2)}, u32[]{:S(2)}) async-start(bf16[16,2,7168]{2,1,0:T(2,128)(2,1)} %reshape.232), calls=%async_computation.1 | async-start | bytes 917504 | tf_op jit(solution)/shard_map/all_to_all | solution.py:103
  78.0 0.8 copy-start.4
  78.8 51.4 %all-to-all-start.5 = ((bf16[16,448,256]{2,1,0:T(8,128)(2,1)}), bf16[16,448,256]{2,1,0:T(8,128)(2,1)}, u32[]{:S(2)}, u32[]{:S(2)}) async-start(bf16[16,448,256]{2,1,0:T(8,128)(2,1)} %get-tuple-element.44), calls=%async_computation.5 | async-start | bytes 7340032 | tf_op jit(solution)/shard_map/all_to_all | solution.py:95
  84.6 130.6 %all-gather.6.cloned.1.call-start = ((), (), s32[]{:S(2)}) async-start(), calls=%async_computation.15 | async-start | bytes 4128768 | tf_op jit(solution)/shard_map/all_gather | solution.py:109
  130.2 9.1 %copy-start.3 = (bf16[8,256,448]{1,2,0:T(8,128)(2,1)S(1)}, bf16[8,256,448]{1,2,0:T(8,128)(2,1)}, u32[]{:S(2)}) copy-start(bf16[8,256,448]{1,2,0:T(8,128)(2,1)} %param.17) | copy-start | bytes 5505028
  130.2 54.6 %all-to-all-start.4 = ((bf16[16,448,256]{2,1,0:T(8,128)(2,1)}), bf16[16,448,256]{2,1,0:T(8,128)(2,1)}, u32[]{:S(2)}, u32[]{:S(2)}) async-start(bf16[16,448,256]{2,1,0:T(8,128)(2,1)} %get-tuple-element.43), calls=%async_computation.4 | async-start | bytes 7340032 | tf_op jit(solution)/shard_map/all_to_all | solution.py:96
  184.7 54.4 %all-to-all-start.2 = ((bf16[16,256,448]{1,2,0:T(8,128)(2,1)}), bf16[16,256,448]{1,2,0:T(8,128)(2,1)}, u32[]{:S(2)}, u32[]{:S(2)}) async-start(bf16[16,256,448]{1,2,0:T(8,128)(2,1)} %broadcast_select_fusion.2), calls=%async_computation.2 | async-start | bytes 7340032 | tf_op jit(solution)/shard_map/all_to_all | solution.py:97
  193.5 95.9 %reduce-scatter.5.cloned.1.call-start = ((), (), s32[]{:S(2)}) async-start(), calls=%async_computation.14 | async-start | bytes 73728 | tf_op jit(solution)/shard_map/reduce_scatter | solution.py:119
  224.9 4.8 copy-start.2
  254.4 169.1 %reduce-scatter.3.cloned.1.call-start = ((), (), s32[]{:S(2)}) async-start(), calls=%async_computation.13 | async-start | bytes 8257536 | tf_op jit(solution)/shard_map/reduce_scatter | solution.py:118
  289.4 15.4 %all-to-all-start.7 = ((f32[1,16,2]{2,0,1:T(1,128)}), f32[1,16,2]{2,0,1:T(1,128)S(1)}, u32[]{:S(2)}, u32[]{:S(2)}) async-start(f32[1,16,2]{2,0,1:T(1,128)} %bitcast.76), calls=%async_computation.9 | async-start | bytes 16384 | tf_op jit(solution)/shard_map/all_to_all | solution.py:123
  304.8 51.5 %all-to-all-start.10 = ((bf16[16,256,448]{1,2,0:T(8,128)(2,1)}), bf16[16,256,448]{1,2,0:T(8,128)(2,1)}, u32[]{:S(2)}, u32[]{:S(2)}) async-start(bf16[16,256,448]{1,2,0:T(8,128)(2,1)} %copy.104), calls=%async_computation.12 | async-start | bytes 7340032 | tf_op jit(solution)/shard_map/all_to_all | solution.py:144
  356.3 54.7 %all-to-all-start.8 = ((bf16[16,448,256]{2,1,0:T(8,128)(2,1)}), bf16[16,448,256]{2,1,0:T(8,128)(2,1)}, u32[]{:S(2)}, u32[]{:S(2)}) async-start(bf16[16,448,256]{2,1,0:T(8,128)(2,1)} %bitcast.72), calls=%async_computation.10 | async-start | bytes 7340032 | tf_op jit(solution)/shard_map/all_to_all | solution.py:142
  411.0 53.4 %all-to-all-start.9 = ((bf16[16,448,256]{2,1,0:T(8,128)(2,1)}), bf16[16,448,256]{2,1,0:T(8,128)(2,1)}, u32[]{:S(2)}, u32[]{:S(2)}) async-start(bf16[16,448,256]{2,1,0:T(8,128)(2,1)} %bitcast.71), calls=%async_computation.11 | async-start | bytes 7340032 | tf_op jit(solution)/shard_map/all_to_all | solution.py:143
  464.4 25.4 %all-to-all-start.6 = ((f32[1,16,2,7168]{3,2,0,1:T(2,128)}), f32[1,16,2,7168]{3,2,0,1:T(2,128)S(1)}, u32[]{:S(2)}, u32[]{:S(2)}) async-start(f32[1,16,2,7168]{3,2,0,1:T(2,128)} %copy.97), calls=%async_computation.7 | async-start | bytes 1835008 | tf_op jit(solution)/shard_map/all_to_all | solution.py:122
  488.2 11.7 %copy-start.1 = (bf16[8,448,256]{2,1,0:T(8,128)(2,1)S(1)}, bf16[8,448,256]{2,1,0:T(8,128)(2,1)}, u32[]{:S(2)}) copy-start(bf16[8,448,256]{2,1,0:T(8,128)(2,1)} %param.16) | copy-start | bytes 5505028
Sparse Core Ops, SparseCore 0:
  45.1 26.5 all-gather.7
  87.7 29.2 all-gather.5
  254.6 30.1 reduce-scatter.4
  287.0 47.4 reduce-scatter.2
where the time goes:
time: 516 us; the launch traced here: 507 us
  waiting for transfers between devices  210 us (41%)
  starting transfers between devices  77.3 us (15%)
  local copies, waits for them, and re-layouts  74.5 us (14%)
  matrix products  72.8 us (14%)
  blocking collectives  30.7 us (6%)
  other arithmetic  27.2 us (5%)
  between operations  14.2 us (3%)
    all_to_all x1, waiting for transfers between devices, local(): lax.all_to_all(copy_gate, 'dev', split_axis=0, concat_axis=0, tiled=True)  44.8 us
    all_to_all x1, waiting for transfers between devices, local(): lax.all_to_all(send_gate, 'dev', split_axis=0, concat_axis=0, tiled=True)  41.6 us
    all_to_all x1, waiting for transfers between devices, local(): lax.all_to_all(send_down, 'dev', split_axis=0, concat_axis=0, tiled=True)  39.1 us
    all_to_all x1, waiting for transfers between devices, local(): lax.all_to_all(copy_up, 'dev', split_axis=0, concat_axis=0, tiled=True)  38.6 us
    all_to_all x1, waiting for transfers between devices, local(): lax.all_to_all(send_up, 'dev', split_axis=0, concat_axis=0, tiled=True)  38.1 us
    reshape x2, local copies, waits for them, and re-layouts, expert_pass(): dy_split = dy_piece.reshape(-1, slot_count, model_width // slot_count)  18.1 us
    reshape x2, local copies, waits for them, and re-layouts, expert_pass(): row_acc = row_terms.reshape(lead_count, slot_count, -1, model_width)  18 us
    all_to_all x1, blocking collectives, local(): lax.all_to_all(x_send, 'dev', split_axis=0, concat_axis=0, tiled=True)  17.7 us
  transfers between devices with their start and end apart: 14, of which 7 were waited for; matrix products, arithmetic and copies ran while one was open for 25% of the time, Pallas kernels for 0%

commit v1 on v0

--- a/solution.py
+++ b/solution.py
@@ -103,11 +103,35 @@
         lax.all_to_all(dy_send, "dev", split_axis=0, concat_axis=0, tiled=True),
         lax.all_to_all(gate_send, "dev", split_axis=0, concat_axis=0, tiled=True),
     )
+
+    def _turn_sectors(w_in):
+        oldest = jax.lax.axis_size("node")
+        left_arr, t1, piece_out = (oldest, jax.lax.axis_index("node"), w_in.shape[0])
+        stack_in = []
+        for kk in [*range(left_arr)]:
+            stack_in.append((kk, (kk + 1) % left_arr))
+        all_blocks = []
+        for kk in tuple(range(left_arr)):
+            all_blocks.append((kk, (kk - 1) % left_arr))
+        w1 = jnp.zeros((*w_in.shape[:0], left_arr * piece_out, *w_in.shape[1:]), w_in.dtype)
+        w1 = lax.dynamic_update_slice_in_dim(w1, w_in, t1 * piece_out, axis=0)
+        f_now = wide_out = w_in
+        near = left_arr // 2
+        for i in [*range(1, near + 1)]:
+            f_now = jax.lax.ppermute(f_now, axis_name="node", perm=stack_in)
+            w1 = lax.dynamic_update_slice_in_dim(w1, f_now, (t1 - i) % left_arr * piece_out, axis=0)
+            if i < left_arr - near:
+                wide_out = jax.lax.ppermute(wide_out, axis_name="node", perm=all_blocks)
+                w1 = lax.dynamic_update_slice_in_dim(
+                    w1, wide_out, (t1 + i) % left_arr * piece_out, axis=0
+                )
+        return w1
+
     totals = expert_pass(
         (
             lax.all_gather(got_x[None], "node", axis=0, tiled=True),
             lax.all_gather(got_dy[None], "node", axis=0, tiled=True),
-            lax.all_gather(got_gate[None], "node", axis=0, tiled=True),
+            _turn_sectors(got_gate[None]),
         ),
         slot_gate,
         slot_up,

time: 516 us -> 525 us (1.017)
  waiting for transfers between devices: 210 us -> 225 us
  blocking collectives: 30.7 us -> 17.7 us
  starting transfers between devices: 77.3 us -> 82.8 us
    all_gather x1 -> x0, blocking collectives: 13 us -> none  [local(): lax.all_gather(got_gate[None], 'node', axis=0, tiled=True)]
    ppermute x0 -> x7, starting transfers between devices: none -> 6.45 us  [the longest x3 5.59 us: _turn_sectors(): wide_out = jax.lax.ppermute(wide_out, axis_name='node', perm=all_blocks)]
    all_to_all x1, waiting for transfers between devices: 38.6 us -> 44.8 us  [local(): lax.all_to_all(copy_up, 'dev', split_axis=0, concat_axis=0, tiled=True)]
    all_to_all x1, waiting for transfers between devices: 41.6 us -> 47.7 us  [local(): lax.all_to_all(send_gate, 'dev', split_axis=0, concat_axis=0, tiled=True)]
    all_to_all x1, waiting for transfers between devices: 44.8 us -> 38.7 us  [local(): lax.all_to_all(copy_gate, 'dev', split_axis=0, concat_axis=0, tiled=True)]
  transfers between devices with their start and end apart: 14 -> 21, of which waited for: 7 -> 15; matrix products, arithmetic and copies ran while one was open for 25% -> 25% of each run, Pallas kernels for 0% -> 0%
where the time goes in v1:
time: 525 us; the launch traced here: 515 us
  waiting for transfers between devices  225 us (43%)
  starting transfers between devices  82.8 us (16%)
  local copies, waits for them, and re-layouts  75.1 us (14%)
  matrix products  72.9 us (14%)
  other arithmetic  26.9 us (5%)
  blocking collectives  17.7 us (3%)
  between operations  14.4 us (3%)
    all_to_all x1, waiting for transfers between devices, local(): lax.all_to_all(send_gate, 'dev', split_axis=0, concat_axis=0, tiled=True)  47.7 us
    all_to_all x1, waiting for transfers between devices, local(): lax.all_to_all(copy_up, 'dev', split_axis=0, concat_axis=0, tiled=True)  44.8 us
    all_to_all x1, waiting for transfers between devices, local(): lax.all_to_all(send_down, 'dev', split_axis=0, concat_axis=0, tiled=True)  40.4 us
    all_to_all x1, waiting for transfers between devices, local(): lax.all_to_all(copy_gate, 'dev', split_axis=0, concat_axis=0, tiled=True)  38.7 us
    all_to_all x1, waiting for transfers between devices, local(): lax.all_to_all(send_up, 'dev', split_axis=0, concat_axis=0, tiled=True)  35.6 us
    reshape x2, local copies, waits for them, and re-layouts, expert_pass(): row_acc = row_terms.reshape(lead_count, slot_count, -1, model_width)  18 us
    reshape x2, local copies, waits for them, and re-layouts, expert_pass(): dy_split = dy_piece.reshape(-1, slot_count, model_width // slot_count)  18 us
    all_to_all x1, blocking collectives, local(): lax.all_to_all(x_send, 'dev', split_axis=0, concat_axis=0, tiled=True)  17.7 us
  transfers between devices with their start and end apart: 21, of which 15 were waited for; matrix products, arithmetic and copies ran while one was open for 25% of the time, Pallas kernels for 0%

profile of v1, /device:TPU:14, one launch (start us, length us, event | category | flops | bytes accessed | tf_op | source)
XLA Modules:
  0.0 515.2 jit_solution(11072962703943981770)
XLA Ops:
  8.9 9.2 %select_reduce_fusion = (s32[256,8]{1,0:T(8,128)S(1)}, s32[256,8]{1,0:T(8,128)S(1)}) fusion(s32[256]{0:T(256)S(1)} %bitcast.79, s32[256,8]{1,0:T(8,128)S(1)} %copy.99, s32[256]{0:T(256)S(1)} %bitcast.78), kind=kLoop, calls=%fused_computation.21 | loop fusion | flops 2617344 | bytes 26624 | tf_op jit(solution)/shard_map/reduce_sum | solution.py:54
  27.2 17.7 %all_to_all.60 = bf16[16,2,7168]{2,1,0:T(2,128)(2,1)} all-to-all(bf16[16,2,7168]{2,1,0:T(2,128)(2,1)S(1)} %reshape.235), channel_id=1, replica_groups=mesh['node'=8,'dev'=16] {'dev'}, dimensions={0} | all-to-all | bytes 917504 | tf_op jit(solution)/shard_map/all_to_all | solution.py:102
  62.2 7.3 %all-to-all-start.1 = ((bf16[16,2,7168]{2,1,0:T(2,128)(2,1)}), bf16[16,2,7168]{2,1,0:T(2,128)(2,1)S(1)}, u32[]{:S(2)}, u32[]{:S(2)}) async-start(bf16[16,2,7168]{2,1,0:T(2,128)(2,1)} %reshape.232), calls=%async_computation.1 | async-start | bytes 917504 | tf_op jit(solution)/shard_map/all_to_all | solution.py:103
  69.5 6.9 %broadcast_select_fusion.1 = (bf16[16,448,256]{2,1,0:T(8,128)(2,1)}, bf16[16,448,256]{2,1,0:T(8,128)(2,1)}) fusion(bf16[16,448,256]{2,1,0:T(8,128)(2,1)} %gather_fusion.1, pred[16]{0:T(512)(128)(4,1)S(1)} %compare_and_fusion, bf16[16,448,256]{2,1,0:T(8,128)(2,1)} %gather_fusion.2), kind=kLoop, calls=%fused_computation.19 | loop fusion | flops 3670016 | bytes 14680080 | tf_op jit(solution)/shard_map/jit(_take)/select_n | solution.py:92
  85.2 44.8 %all-to-all-done.4 = bf16[16,448,256]{2,1,0:T(8,128)(2,1)} async-done(((bf16[16,448,256]{2,1,0:T(8,128)(2,1)}), bf16[16,448,256]{2,1,0:T(8,128)(2,1)}, u32[]{:S(2)}, u32[]{:S(2)}) %all-to-all-start.4) | async-done | bytes 3670048 | tf_op jit(solution)/shard_map/all_to_all | solution.py:96
  130.0 9.0 %all-to-all-start.5 = ((bf16[16,448,256]{2,1,0:T(8,128)(2,1)}), bf16[16,448,256]{2,1,0:T(8,128)(2,1)}, u32[]{:S(2)}, u32[]{:S(2)}) async-start(bf16[16,448,256]{2,1,0:T(8,128)(2,1)} %get-tuple-element.39), calls=%async_computation.5 | async-start | bytes 7340032 | tf_op jit(solution)/shard_map/all_to_all | solution.py:95
  145.9 38.7 %all-to-all-done.5 = bf16[16,448,256]{2,1,0:T(8,128)(2,1)} async-done(((bf16[16,448,256]{2,1,0:T(8,128)(2,1)}), bf16[16,448,256]{2,1,0:T(8,128)(2,1)}, u32[]{:S(2)}, u32[]{:S(2)}) %all-to-all-start.5) | async-done | bytes 3670048 | tf_op jit(solution)/shard_map/all_to_all | solution.py:95
  184.6 8.8 %all-to-all-start.2 = ((bf16[16,256,448]{1,2,0:T(8,128)(2,1)}), bf16[16,256,448]{1,2,0:T(8,128)(2,1)}, u32[]{:S(2)}, u32[]{:S(2)}) async-start(bf16[16,256,448]{1,2,0:T(8,128)(2,1)} %broadcast_select_fusion.2), calls=%async_computation.2 | async-start | bytes 7340032 | tf_op jit(solution)/shard_map/all_to_all | solution.py:97
  206.4 8.4 %reshape.236 = bf16[256,7168]{1,0:T(8,128)(2,1)} reshape(bf16[128,2,7168]{2,1,0:T(2,128)(2,1)} %all-gather.7.cloned.1.call-done) | data formatting | bytes 7340032 | tf_op jit(solution)/shard_map/reshape | solution.py:16
  214.8 9.6 %reshape.233 = bf16[256,16,448]{2,1,0:T(8,128)(2,1)} reshape(bf16[128,2,7168]{2,1,0:T(2,128)(2,1)} %all-gather.5.cloned.1.call-done) | data formatting | bytes 7340032 | tf_op jit(solution)/shard_map/reshape | solution.py:17
  238.9 8.3 %multiply_reduce_fusion = (f32[256]{0:T(256)S(1)}, bf16[256,256]{0,1:T(8,128)(2,1)S(1)}, bf16[256,256]{0,1:T(8,128)(2,1)S(1)}) fusion(f32[256,256]{0,1:T(8,128)S(1)} %fusion.61, f32[256,256]{0,1:T(8,128)S(1)} %fusion.62, f32[256]{0:T(256)S(1)} %reshape.245, bf16[16,256,448]{1,2,0:T(8,128)(2,1)} %all-to-all-done.2, bf16[256,16,448]{2,1,0:T(8,128)(2,1)} %reshape.233), kind=kOutput, calls=%fused_computation.32 | convolution fusion | flops 940637952 | bytes 8128512 | tf_op jit(solution)/shard_map/rsk,shk->rh/dot_general | solution.py:21
  254.2 8.3 %convolution_add_fusion = f32[256,7168]{1,0:T(8,128)} fusion(f32[256,7168]{1,0:T(8,128)} %fusion.63, bf16[256,256]{0,1:T(8,128)(2,1)S(1)} %get-tuple-element.35, bf16[7168,256]{1,0:T(8,128)(2,1)} %bitcast.10), kind=kOutput, calls=%fused_computation.3 | convolution fusion | flops 941359104 | bytes 18481152 | tf_op jit(solution)/shard_map/rh,dh->rd/dot_general | solution.py:33
  262.5 9.7 %reshape.239 = f32[8,16,2,7168]{3,2,1,0:T(2,128)} reshape(f32[256,7168]{1,0:T(8,128)} %convolution_add_fusion) | data formatting | bytes 14680064 | tf_op jit(solution)/shard_map/reshape | solution.py:41
  272.3 8.2 %copy.114 = f32[8,16,2,7168]{3,1,2,0:T(8,128)} copy(f32[8,16,2,7168]{3,2,1,0:T(2,128)} %reshape.239) | data formatting | bytes 14680064 | tf_op jit(solution)/shard_map/reshape | solution.py:41
  284.6 7.4 %all-to-all-start.7 = ((f32[1,16,2]{2,0,1:T(1,128)}), f32[1,16,2]{2,0,1:T(1,128)S(1)}, u32[]{:S(2)}, u32[]{:S(2)}) async-start(f32[1,16,2]{2,0,1:T(1,128)} %bitcast.77), calls=%async_computation.9 | async-start | bytes 16384 | tf_op jit(solution)/shard_map/all_to_all | solution.py:147
  298.1 6.3 %all-to-all-start.8 = ((bf16[16,448,256]{2,1,0:T(8,128)(2,1)}), bf16[16,448,256]{2,1,0:T(8,128)(2,1)}, u32[]{:S(2)}, u32[]{:S(2)}) async-start(bf16[16,448,256]{2,1,0:T(8,128)(2,1)} %bitcast.73), calls=%async_computation.10 | async-start | bytes 7340032 | tf_op jit(solution)/shard_map/all_to_all | solution.py:166
  309.6 47.7 %all-to-all-done.8 = bf16[16,448,256]{2,1,0:T(8,128)(2,1)} async-done(((bf16[16,448,256]{2,1,0:T(8,128)(2,1)}), bf16[16,448,256]{2,1,0:T(8,128)(2,1)}, u32[]{:S(2)}, u32[]{:S(2)}) %all-to-all-start.8) | async-done | bytes 3670048 | tf_op jit(solution)/shard_map/all_to_all | solution.py:166
  357.2 8.8 %all-to-all-start.9 = ((bf16[16,448,256]{2,1,0:T(8,128)(2,1)}), bf16[16,448,256]{2,1,0:T(8,128)(2,1)}, u32[]{:S(2)}, u32[]{:S(2)}) async-start(bf16[16,448,256]{2,1,0:T(8,128)(2,1)} %bitcast.72), calls=%async_computation.11 | async-start | bytes 7340032 | tf_op jit(solution)/shard_map/all_to_all | solution.py:167
  366.0 8.4 %copy.121 = bf16[256,16,448]{0,1,2:T(8,128)(2,1)} copy(bf16[256,16,448]{2,1,0:T(8,128)(2,1)} %reshape.233) | data formatting | bytes 7340032 | tf_op jit(solution)/shard_map/reshape | solution.py:17
  380.9 35.6 %all-to-all-done.9 = bf16[16,448,256]{2,1,0:T(8,128)(2,1)} async-done(((bf16[16,448,256]{2,1,0:T(8,128)(2,1)}), bf16[16,448,256]{2,1,0:T(8,128)(2,1)}, u32[]{:S(2)}, u32[]{:S(2)}) %all-to-all-start.9) | async-done | bytes 3670048 | tf_op jit(solution)/shard_map/all_to_all | solution.py:167
  416.5 9.0 %all-to-all-start.10 = ((bf16[16,256,448]{1,2,0:T(8,128)(2,1)}), bf16[16,256,448]{1,2,0:T(8,128)(2,1)}, u32[]{:S(2)}, u32[]{:S(2)}) async-start(bf16[16,256,448]{1,2,0:T(8,128)(2,1)} %copy.122), calls=%async_computation.12 | async-start | bytes 7340032 | tf_op jit(solution)/shard_map/all_to_all | solution.py:168
  431.5 40.4 %all-to-all-done.10 = bf16[16,256,448]{1,2,0:T(8,128)(2,1)} async-done(((bf16[16,256,448]{1,2,0:T(8,128)(2,1)}), bf16[16,256,448]{1,2,0:T(8,128)(2,1)}, u32[]{:S(2)}, u32[]{:S(2)}) %all-to-all-start.10) | async-done | bytes 3670048 | tf_op jit(solution)/shard_map/all_to_all | solution.py:168
  471.9 9.0 %all-to-all-start.6 = ((f32[1,16,2,7168]{3,2,0,1:T(2,128)}), f32[1,16,2,7168]{3,2,0,1:T(2,128)S(1)}, u32[]{:S(2)}, u32[]{:S(2)}) async-start(f32[1,16,2,7168]{3,2,0,1:T(2,128)} %copy.115), calls=%async_computation.7 | async-start | bytes 1835008 | tf_op jit(solution)/shard_map/all_to_all | solution.py:146
  499.9 8.5 %convolution_convert_fusion.2 = bf16[256,7168]{1,0:T(8,128)(2,1)} fusion(f32[32,256]{1,0:T(8,128)S(1)} %convert_reduce_fusion, f32[32,7168]{1,0:T(8,128)} %reshape.240), kind=kOutput, calls=%fused_computation.6 | convolution fusion | flops 706478080 | bytes 4620288 | tf_op jit(solution)/shard_map/qt,qd->td/dot_general | solution.py:149
  (131 shorter events, 124.8 us)
Async XLA Ops:
  7.2 44.6 %copy-start = (bf16[8,448,256]{2,1,0:T(8,128)(2,1)S(1)}, bf16[8,448,256]{2,1,0:T(8,128)(2,1)}, u32[]{:S(2)}) copy-start(bf16[8,448,256]{2,1,0:T(8,128)(2,1)} %param.16) | copy-start | bytes 5505028
  7.2 199.3 %all-gather.7.cloned.1.call-start = ((), (), s32[]{:S(2)}) async-start(), calls=%async_computation.16 | async-start | bytes 4128768 | tf_op jit(solution)/shard_map/all_gather | solution.py:132
  23.9 21.2 %copy-start.6 = (bf16[256,8]{0,1:T(8,128)(2,1)S(1)}, bf16[256,8]{0,1:T(8,128)(2,1)}, u32[]{:S(2)}) copy-start(bf16[256,8]{0,1:T(8,128)(2,1)} %param.12) | copy-start | bytes 12292
  24.0 26.9 %copy-start.5 = (s32[256,2]{0,1:T(2,128)S(1)}, s32[256,2]{0,1:T(2,128)}, u32[]{:S(2)}) copy-start(s32[256,2]{0,1:T(2,128)} %param.14) | copy-start | bytes 6148
  46.2 16.0 %all-to-all-start = ((bf16[16,1,2]{2,1,0:T(2,128)(2,1)}), bf16[16,1,2]{2,1,0:T(2,128)(2,1)S(1)}, u32[]{:S(2)}, u32[]{:S(2)}) async-start(bf16[16,1,2]{2,1,0:T(2,128)(2,1)} %all_to_all.48), calls=%async_computation | async-start | bytes 16384 | tf_op jit(solution)/shard_map/all_to_all | solution.py:104
  62.2 15.7 %all-to-all-start.1 = ((bf16[16,2,7168]{2,1,0:T(2,128)(2,1)}), bf16[16,2,7168]{2,1,0:T(2,128)(2,1)S(1)}, u32[]{:S(2)}, u32[]{:S(2)}) async-start(bf16[16,2,7168]{2,1,0:T(2,128)(2,1)} %reshape.232), calls=%async_computation.1 | async-start | bytes 917504 | tf_op jit(solution)/shard_map/all_to_all | solution.py:103
  78.7 51.3 %all-to-all-start.4 = ((bf16[16,448,256]{2,1,0:T(8,128)(2,1)}), bf16[16,448,256]{2,1,0:T(8,128)(2,1)}, u32[]{:S(2)}, u32[]{:S(2)}) async-start(bf16[16,448,256]{2,1,0:T(8,128)(2,1)} %get-tuple-element.38), calls=%async_computation.4 | async-start | bytes 7340032 | tf_op jit(solution)/shard_map/all_to_all | solution.py:96
  84.5 130.4 %all-gather.5.cloned.1.call-start = ((), (), s32[]{:S(2)}) async-start(), calls=%async_computation.15 | async-start | bytes 4128768 | tf_op jit(solution)/shard_map/all_gather | solution.py:133
  130.0 54.6 %all-to-all-start.5 = ((bf16[16,448,256]{2,1,0:T(8,128)(2,1)}), bf16[16,448,256]{2,1,0:T(8,128)(2,1)}, u32[]{:S(2)}, u32[]{:S(2)}) async-start(bf16[16,448,256]{2,1,0:T(8,128)(2,1)} %get-tuple-element.39), calls=%async_computation.5 | async-start | bytes 7340032 | tf_op jit(solution)/shard_map/all_to_all | solution.py:95
  184.6 54.3 %all-to-all-start.2 = ((bf16[16,256,448]{1,2,0:T(8,128)(2,1)}), bf16[16,256,448]{1,2,0:T(8,128)(2,1)}, u32[]{:S(2)}, u32[]{:S(2)}) async-start(bf16[16,256,448]{1,2,0:T(8,128)(2,1)} %broadcast_select_fusion.2), calls=%async_computation.2 | async-start | bytes 7340032 | tf_op jit(solution)/shard_map/all_to_all | solution.py:97
  193.3 91.3 %reduce-scatter.5.cloned.1.call-start = ((), (), s32[]{:S(2)}) async-start(), calls=%async_computation.14 | async-start | bytes 73728 | tf_op jit(solution)/shard_map/reduce_scatter | solution.py:143
  193.9 3.0 collective-permute-start
  193.9 3.1 collective-permute-start.1
  197.0 3.0 collective-permute-start.2
  197.1 3.0 collective-permute-start.3
  200.1 3.0 collective-permute-start.4
  200.2 4.3 collective-permute-start.5
  203.2 3.0 collective-permute-start.6
  254.1 174.6 %reduce-scatter.3.cloned.1.call-start = ((), (), s32[]{:S(2)}) async-start(), calls=%async_computation.13 | async-start | bytes 8257536 | tf_op jit(solution)/shard_map/reduce_scatter | solution.py:142
  284.6 13.5 %all-to-all-start.7 = ((f32[1,16,2]{2,0,1:T(1,128)}), f32[1,16,2]{2,0,1:T(1,128)S(1)}, u32[]{:S(2)}, u32[]{:S(2)}) async-start(f32[1,16,2]{2,0,1:T(1,128)} %bitcast.77), calls=%async_computation.9 | async-start | bytes 16384 | tf_op jit(solution)/shard_map/all_to_all | solution.py:147
  298.1 59.1 %all-to-all-start.8 = ((bf16[16,448,256]{2,1,0:T(8,128)(2,1)}), bf16[16,448,256]{2,1,0:T(8,128)(2,1)}, u32[]{:S(2)}, u32[]{:S(2)}) async-start(bf16[16,448,256]{2,1,0:T(8,128)(2,1)} %bitcast.73), calls=%async_computation.10 | async-start | bytes 7340032 | tf_op jit(solution)/shard_map/all_to_all | solution.py:166
  357.2 59.3 %all-to-all-start.9 = ((bf16[16,448,256]{2,1,0:T(8,128)(2,1)}), bf16[16,448,256]{2,1,0:T(8,128)(2,1)}, u32[]{:S(2)}, u32[]{:S(2)}) async-start(bf16[16,448,256]{2,1,0:T(8,128)(2,1)} %bitcast.72), calls=%async_computation.11 | async-start | bytes 7340032 | tf_op jit(solution)/shard_map/all_to_all | solution.py:167
  416.5 55.4 %all-to-all-start.10 = ((bf16[16,256,448]{1,2,0:T(8,128)(2,1)}), bf16[16,256,448]{1,2,0:T(8,128)(2,1)}, u32[]{:S(2)}, u32[]{:S(2)}) async-start(bf16[16,256,448]{1,2,0:T(8,128)(2,1)} %copy.122), calls=%async_computation.12 | async-start | bytes 7340032 | tf_op jit(solution)/shard_map/all_to_all | solution.py:168
  471.9 26.5 %all-to-all-start.6 = ((f32[1,16,2,7168]{3,2,0,1:T(2,128)}), f32[1,16,2,7168]{3,2,0,1:T(2,128)S(1)}, u32[]{:S(2)}, u32[]{:S(2)}) async-start(f32[1,16,2,7168]{3,2,0,1:T(2,128)} %copy.115), calls=%async_computation.7 | async-start | bytes 1835008 | tf_op jit(solution)/shard_map/all_to_all | solution.py:146
  (4 other events, 26.3 us)
Sparse Core Ops, SparseCore 0:
  45.1 26.5 all-gather.6
  87.5 29.2 all-gather.4
  254.3 30.3 reduce-scatter.4
  286.9 47.3 reduce-scatter.2
